TPU v7x, 512 devices: a whole 4x4x16 slice. The times are simulated.
512 devices in a mesh: dp: 32 (over z, core), seq: 16 (over x, y).
Axes of the slice: x: 4, y: 4, z: 16, core: 2. Of those that a mesh axis runs over, the one named last changes fastest.
Arguments:
- queries: bfloat16 [65536, 4096], P(('dp', 'seq')), may hold values from -9 to 9
- keys: bfloat16 [65536, 512], P(('dp', 'seq')), may hold values from -9 to 9
- values: bfloat16 [65536, 512], P(('dp', 'seq')), may hold values from -6 to 6
- grad_out: bfloat16 [65536, 4096], P(('dp', 'seq')), may hold values from -6 to 6
- doc_lengths: int32 [32, 32], replicated, may hold values from 1 to 128, 2048 in all within a row
- swap_mask: int32 [1], replicated, may hold values from 1 to 31
Outputs:
- grad_query: bfloat16 [65536, 4096], P(('dp', 'seq'))
- grad_key: bfloat16 [65536, 512], P(('dp', 'seq'))
- grad_value: bfloat16 [65536, 512], P(('dp', 'seq'))
Inputs may be any that keep to these rules, and one draw needn't show every extreme that they name: `doc_lengths`: row p holds the lengths of the 32 documents of pack p in order; they sum to 2048 and the longest is 128. `swap_mask`: never zero.
All inputs are finite; a program needn't handle non-finite values.
Results may differ from a plain program's by a relative error of at most 0.0071.
Values may be sent and summed in bfloat16 or wider, within the bound.
No kernel may reach another device: no remote copies, remote signals or barrier semaphores. Data moves between devices by JAX's collectives and lax.ppermute only.
A program may use at most 64 MiB of HBM per device.

v0:
```python
import jax
import jax.numpy as jnp
from jax import lax
from jax.sharding import PartitionSpec as P

HQ = 32
KV = 4
DH = 128
MOST = 128


contract_last = (((1,), (1,)), ((), ()))
contract_inner = (((1,), (0,)), ((), ()))
contract_first = (((0,), (0,)), ((), ()))


def in_one_piece(arrays, axis, split_dim, concat_dim, along):
    both = jnp.concatenate(arrays, axis=along)
    result, at, gathered = (
        lax.all_to_all(both, axis, split_axis=split_dim, concat_axis=concat_dim, tiled=True),
        0,
        [],
    )
    for a in arrays:
        gathered.append(lax.slice_in_dim(result, at, at + a.shape[along], axis=along))
        at += a.shape[along]
    return tuple(gathered)


def shortened(x):

    def short(part):
        return part.astype(jnp.bfloat16) if part.dtype == jnp.float32 else part

    return jax.tree.map(short, x)


def from_partner(block, axis, stride):
    count = lax.axis_size(axis)
    route = []
    for low in range(count):
        high = low | 1 << stride
        if high != low and high < count:
            route += [(low, high), (high, low)]
    return lax.ppermute(block, axis, route)


def product(left, right, dims):
    return lax.dot_general(left, right, dims, preferred_element_type=jnp.float32)


def head_grads(query_one, grad_one, key_one, value_one, segment, width):
    length = query_one.shape[0]
    scale = DH ** (-0.5)
    positions = jnp.arange(length, dtype=jnp.int32)
    dq_parts = []
    dk_total = jnp.zeros((length, DH), jnp.float32)
    dv_total = jnp.zeros((length, DH), jnp.float32)
    for i in range(length // width):
        lower = i * width
        upper = lower + width
        key_start = max(0, lower - MOST)
        query_block = query_one[lower:upper]
        grad_block = grad_one[lower:upper]
        key_band = key_one[key_start:upper]
        value_band = value_one[key_start:upper]
        scores = product(query_block, key_band, contract_last)
        dprobs = product(grad_block, value_band, contract_last)
        allowed = (positions[None, key_start:upper] <= positions[lower:upper, None]) & (
            segment[None, key_start:upper] == segment[lower:upper, None]
        )
        scores = jnp.where(allowed, scores * scale, -1e30)
        peak = jnp.max(scores, axis=1, keepdims=True)
        expo = jnp.where(allowed, jnp.exp(scores - peak), 0.0)
        probs = expo / jnp.sum(expo, axis=1, keepdims=True)
        probs_low = probs.astype(jnp.bfloat16)
        delta = jnp.sum(probs * dprobs, axis=1, keepdims=True)
        dscores = (probs * (dprobs - delta)).astype(jnp.bfloat16)
        dq_block = product(dscores, key_band, contract_inner)
        dk_rows = product(dscores, query_block, contract_first)
        dv_rows = product(probs_low, grad_block, contract_first)
        dq_parts.append((dq_block * scale).astype(jnp.bfloat16))
        dk_total = dk_total.at[key_start:upper].add(dk_rows * scale)
        dv_total = dv_total.at[key_start:upper].add(dv_rows)
    return (jnp.concatenate(dq_parts, axis=0), dk_total, dv_total)


def body(queries, keys, values, grad_out, doc_lengths, swap_mask):
    seq_count = lax.axis_size("seq")
    local_rows = queries.shape[0]
    pack_rows = local_rows * seq_count
    heads_dev = HQ // seq_count
    group = HQ // KV
    per_kv = min(heads_dev, group)
    width = min(256, pack_rows)
    query_split = queries.reshape(local_rows, seq_count, heads_dev * DH)
    grad_split = grad_out.reshape(local_rows, seq_count, heads_dev * DH)
    query_heads, grad_heads = (
        lax.all_to_all(query_split, "seq", split_axis=1, concat_axis=0, tiled=True),
        lax.all_to_all(grad_split, "seq", split_axis=1, concat_axis=0, tiled=True),
    )
    query_heads = query_heads.reshape(pack_rows, heads_dev, DH)
    grad_heads = grad_heads.reshape(pack_rows, heads_dev, DH)
    repeats = max(1, group // heads_dev)
    key_slots = jnp.repeat(keys.reshape(local_rows, KV, DH), repeats, axis=1)
    value_slots = jnp.repeat(values.reshape(local_rows, KV, DH), repeats, axis=1)
    key_heads, value_heads = in_one_piece((key_slots, value_slots), "seq", 1, 0, 2)
    own_lengths = lax.dynamic_slice_in_dim(doc_lengths, lax.axis_index("dp"), 1, 0)[0]
    ends = jnp.cumsum(own_lengths)
    positions = jnp.arange(pack_rows, dtype=jnp.int32)
    segment = jnp.sum((ends[None, :] <= positions[:, None]).astype(jnp.int32), axis=1)
    dq_list = []
    dk_sums = [jnp.zeros((pack_rows, DH), jnp.float32)]
    dv_sums = [jnp.zeros((pack_rows, DH), jnp.float32)]
    for h in range(heads_dev):
        owner = h // per_kv
        dq_one, dk_one, dv_one = head_grads(
            query_heads[:, h],
            grad_heads[:, h],
            key_heads[:, owner],
            value_heads[:, owner],
            segment,
            width,
        )
        dq_list.append(dq_one)
        dk_sums[owner] = dk_sums[owner] + dk_one
        dv_sums[owner] = dv_sums[owner] + dv_one
    dq_stack = jnp.stack(dq_list, axis=1).reshape(pack_rows, 1, heads_dev * DH)
    dq_back = lax.all_to_all(dq_stack, "seq", split_axis=0, concat_axis=1, tiled=True).reshape(
        local_rows, HQ * DH
    )
    dk_stack = jnp.stack(dk_sums, axis=1)
    dv_stack = jnp.stack(dv_sums, axis=1)
    dk_back, dv_back = (
        lax.all_to_all(dk_stack, "seq", split_axis=0, concat_axis=1, tiled=True),
        lax.all_to_all(dv_stack, "seq", split_axis=0, concat_axis=1, tiled=True),
    )
    dk_local = (
        jnp.sum(dk_back.reshape(local_rows, KV, -1, DH), axis=2)
        .reshape(local_rows, KV * DH)
        .astype(jnp.bfloat16)
    )
    dv_local = (
        jnp.sum(dv_back.reshape(local_rows, KV, -1, DH), axis=2)
        .reshape(local_rows, KV * DH)
        .astype(jnp.bfloat16)
    )
    result = (dq_back, dk_local, dv_local)
    levels = lax.axis_size("dp").bit_length() - 1
    for bit in range(levels):
        flag = jnp.bitwise_and(jnp.right_shift(swap_mask[0], bit), 1) == 1
        result = lax.cond(
            flag,
            lambda carried: jax.tree.map(
                lambda part, own: part.astype(own.dtype),
                from_partner(shortened(carried), "dp", bit),
                carried,
            ),
            lambda carried: carried,
            result,
        )
    return result


def solution(mesh):
    return jax.shard_map(
        body,
        mesh=mesh,
        in_specs=(
            P(("dp", "seq"), None),
            P(("dp", "seq"), None),
            P(("dp", "seq"), None),
            P(("dp", "seq"), None),
            P(),
            P(),
        ),
        out_specs=(P(("dp", "seq"), None), P(("dp", "seq"), None), P(("dp", "seq"), None)),
        check_vma=False,
    )
```

profile of v0, /device:TPU:1, one launch (start us, length us, event | category | flops | bytes accessed | tf_op | source)
XLA Modules:
  0.0 367.7 jit_solution(1737285257640856935)
XLA Ops:
  0.7 2.4 copy.198
  3.0 7.7 %all-to-all-start.1 = ((bf16[128,16,256]{0,2,1:T(8,128)(2,1)}), bf16[128,16,256]{0,2,1:T(8,128)(2,1)S(1)}, u32[]{:S(2)}, u32[]{:S(2)}) async-start(bf16[128,16,256]{0,2,1:T(8,128)(2,1)} %bitcast.12), calls=%async_computation.1 | async-start | bytes 2097152 | tf_op jit(solution)/shard_map/all_to_all | solution.py:99
  13.5 1.3 copy.201
  15.7 1.1 pad_maximum_fusion
  16.8 8.2 %all-to-all-done.1 = bf16[128,16,256]{0,2,1:T(8,128)(2,1)S(1)} async-done(((bf16[128,16,256]{0,2,1:T(8,128)(2,1)}), bf16[128,16,256]{0,2,1:T(8,128)(2,1)S(1)}, u32[]{:S(2)}, u32[]{:S(2)}) %all-to-all-start.1) | async-done | bytes 1048608 | tf_op jit(solution)/shard_map/all_to_all | solution.py:99
  25.0 5.3 %all-to-all-start = ((bf16[128,16,256]{2,0,1:T(8,128)(2,1)}), bf16[128,16,256]{2,0,1:T(8,128)(2,1)S(1)}, u32[]{:S(2)}, u32[]{:S(2)}) async-start(bf16[128,16,256]{2,0,1:T(8,128)(2,1)} %pad_maximum_fusion), calls=%async_computation | async-start | bytes 2097152 | tf_op jit(solution)/shard_map/all_to_all | solution.py:20
  32.9 12.4 %all-to-all-done = bf16[128,16,256]{2,0,1:T(8,128)(2,1)S(1)} async-done(((bf16[128,16,256]{2,0,1:T(8,128)(2,1)}), bf16[128,16,256]{2,0,1:T(8,128)(2,1)S(1)}, u32[]{:S(2)}, u32[]{:S(2)}) %all-to-all-start) | async-done | bytes 1048608 | tf_op jit(solution)/shard_map/all_to_all | solution.py:20
  45.4 4.4 %all-to-all-start.2 = ((bf16[128,16,256]{0,2,1:T(8,128)(2,1)}), bf16[128,16,256]{0,2,1:T(8,128)(2,1)S(1)}, u32[]{:S(2)}, u32[]{:S(2)}) async-start(bf16[128,16,256]{0,2,1:T(8,128)(2,1)} %bitcast.20), calls=%async_computation.2 | async-start | bytes 2097152 | tf_op jit(solution)/shard_map/all_to_all | solution.py:100
  49.8 1.5 fusion.190
  51.3 1.5 fusion.189
  52.9 1.6 fusion.188
  54.4 1.6 fusion.187
  56.0 1.6 fusion.186
  57.6 1.6 fusion.185
  59.1 1.6 fusion.184
  60.7 1.5 fusion.183
  62.2 1.5 fusion.182
  63.8 1.5 fusion.181
  65.4 1.4 fusion.176
  66.8 1.5 fusion.175
  68.3 1.5 fusion.180
  69.8 1.5 fusion.179
  71.4 1.6 fusion.178
  72.9 1.6 fusion.177
  75.9 1.1 fusion.149
  77.0 1.7 fusion.154
  78.7 1.2 multiply_reduce_fusion.15
  98.2 1.4 reduce.65
  100.2 1.1 reshape.1002
  101.3 6.8 %all-to-all-start.3 = ((bf16[16,2,16384]{2,1,0:T(2,128)(2,1)}), bf16[16,2,16384]{2,1,0:T(2,128)(2,1)S(1)}, u32[]{:S(2)}, u32[]{:S(2)}) async-start(bf16[16,2,16384]{2,1,0:T(2,128)(2,1)} %reshape.1002), calls=%async_computation.3 | async-start | bytes 2097152 | tf_op jit(solution)/shard_map/all_to_all | solution.py:129
  108.2 1.2 fusion.59
  116.5 1.1 add.248
  119.4 3.1 all-to-all-done.3
  122.5 5.4 %all-to-all-start.4 = ((f32[2048,1,128]{2,1,0:T(1,128)}), f32[2048,1,128]{2,1,0:T(1,128)}, u32[]{:S(2)}, u32[]{:S(2)}) async-start(f32[2048,1,128]{2,1,0:T(1,128)} %bitcast.105), calls=%async_computation.4 | async-start | bytes 2097152 | tf_op jit(solution)/shard_map/all_to_all | solution.py:135
  127.9 1.4 fusion.42
  129.3 1.2 fusion.41
  130.6 1.1 fusion.40
  131.7 1.1 fusion.39
  132.9 1.1 add.263
  134.0 8.5 %all-to-all-done.4 = f32[2048,1,128]{2,1,0:T(1,128)} async-done(((f32[2048,1,128]{2,1,0:T(1,128)}), f32[2048,1,128]{2,1,0:T(1,128)}, u32[]{:S(2)}, u32[]{:S(2)}) %all-to-all-start.4) | async-done | bytes 1048608 | tf_op jit(solution)/shard_map/all_to_all | solution.py:135
  142.5 5.0 %all-to-all-start.5 = ((f32[2048,1,128]{2,1,0:T(1,128)}), f32[2048,1,128]{2,1,0:T(1,128)}, u32[]{:S(2)}, u32[]{:S(2)}) async-start(f32[2048,1,128]{2,1,0:T(1,128)} %bitcast.111), calls=%async_computation.5 | async-start | bytes 2097152 | tf_op jit(solution)/shard_map/all_to_all | solution.py:136
  150.1 1.3 reduce_sum.348
  151.6 10.5 %all-to-all-done.5 = f32[2048,1,128]{2,1,0:T(1,128)} async-done(((f32[2048,1,128]{2,1,0:T(1,128)}), f32[2048,1,128]{2,1,0:T(1,128)}, u32[]{:S(2)}, u32[]{:S(2)}) %all-to-all-start.5) | async-done | bytes 1048608 | tf_op jit(solution)/shard_map/all_to_all | solution.py:136
  162.1 1.3 reduce_sum.349
  163.5 11.7 %conditional.5 = (bf16[128,4096]{1,0:T(8,128)(2,1)}, bf16[128,512]{1,0:T(8,128)(2,1)}, bf16[128,512]{1,0:T(8,128)(2,1)}) conditional(s32[]{:T(128)} %bitcast.4, (bf16[128,4096]{0,1:T(8,128)(2,1)S(1)}, bf16[128,512]{0,1:T(8,128)(2,1)S(1)}, bf16[128,512]{0,1:T(8,128)(2,1)S(1)}) %tuple.265, (bf16[128,4096]{0,1:T(8,128)(2,1)S(1)}, ...), branch_computations={%region_52.53_spmd, %region_53.54_spmd} | conditional | bytes 7864464 | solution.py:152
  164.1 5.5 %collective-permute-start = (bf16[128,4096]{1,0:T(8,128)(2,1)S(1)}, bf16[128,4096]{1,0:T(8,128)(2,1)}, u32[]{:S(2)}, u32[]{:S(2)}) collective-permute-start(bf16[128,4096]{1,0:T(8,128)(2,1)S(1)} %copy.244), channel_id=1, source_target_pairs={{0,16},{16,0},{32,48},{48,32},{64,80},{80,64},{96,112},{112,96},{1... | collective-permute-start | bytes 3145736 | tf_op jit(solution)/shard_map/cond/branch_1_fun/ppermute | solution.py:45
  169.7 1.9 collective-permute-start.1
  171.7 2.4 collective-permute-start.2
  174.2 1.1 collective-permute-done.2
  175.3 63.7 %conditional.7 = ((bf16[128,4096]{1,0:T(8,128)(2,1)}, bf16[128,512]{1,0:T(8,128)(2,1)}, bf16[128,512]{1,0:T(8,128)(2,1)})) conditional(s32[]{:T(128)} %bitcast.2, (bf16[128,4096]{1,0:T(8,128)(2,1)}, bf16[128,512]{1,0:T(8,128)(2,1)}, bf16[128,512]{1,0:T(8,128)(2,1)}) %get-tuple-element.630, (bf16[128,4096]{1,0:T(8,128)(2,1)}, ...), branch_computations={%region_56.57_spmd, %region_57.58_spmd} | conditional | bytes 7864472 | solution.py:152
  175.3 5.0 %collective-permute-start.6 = (bf16[128,4096]{1,0:T(8,128)(2,1)}, bf16[128,4096]{1,0:T(8,128)(2,1)S(1)}, u32[]{:S(2)}, u32[]{:S(2)}) collective-permute-start(bf16[128,4096]{1,0:T(8,128)(2,1)} %get-tuple-element.450), channel_id=1, source_target_pairs={{0,64},{64,0},{16,80},{80,16},{32,96},{96,32},{48,112},{112,48},{1... | collective-permute-start | bytes 3145736 | tf_op jit(solution)/shard_map/cond/branch_1_fun/ppermute | solution.py:45
  180.3 1.9 collective-permute-start.7
  182.2 4.3 %collective-permute-start.8 = (bf16[128,512]{1,0:T(8,128)(2,1)}, bf16[128,512]{1,0:T(8,128)(2,1)S(1)}, u32[]{:S(2)}, u32[]{:S(2)}) collective-permute-start(bf16[128,512]{1,0:T(8,128)(2,1)} %get-tuple-element.452), channel_id=1, source_target_pairs={{0,64},{64,0},{16,80},{80,16},{32,96},{96,32},{48,112},{112,48},{1... | collective-permute-start | bytes 393224 | tf_op jit(solution)/shard_map/cond/branch_1_fun/ppermute | solution.py:45
  186.5 48.1 %collective-permute-done.7 = bf16[128,512]{1,0:T(8,128)(2,1)S(1)} collective-permute-done((bf16[128,512]{1,0:T(8,128)(2,1)}, bf16[128,512]{1,0:T(8,128)(2,1)S(1)}, u32[]{:S(2)}, u32[]{:S(2)}) %collective-permute-start.7) | collective-permute-done | bytes 131104 | tf_op jit(solution)/shard_map/cond/branch_1_fun/ppermute | solution.py:45
  235.2 2.2 collective-permute-done.8
  239.0 123.2 %conditional.8 = ((bf16[128,4096]{1,0:T(8,128)(2,1)}, bf16[128,512]{1,0:T(8,128)(2,1)}, bf16[128,512]{1,0:T(8,128)(2,1)})) conditional(s32[]{:T(128)} %bitcast.1, (bf16[128,4096]{1,0:T(8,128)(2,1)}, bf16[128,512]{1,0:T(8,128)(2,1)}, bf16[128,512]{1,0:T(8,128)(2,1)}) %get-tuple-element.631, (bf16[128,4096]{1,0:T(8,128)(2,1)}, ...), branch_computations={%region_58.59_spmd, %region_59.60_spmd} | conditional | bytes 7864472 | solution.py:152
  239.0 8.8 %collective-permute-start.9 = (bf16[128,4096]{1,0:T(8,128)(2,1)}, bf16[128,4096]{1,0:T(8,128)(2,1)S(1)}, u32[]{:S(2)}, u32[]{:S(2)}) collective-permute-start(bf16[128,4096]{1,0:T(8,128)(2,1)} %get-tuple-element.453), channel_id=1, source_target_pairs={{0,128},{128,0},{16,144},{144,16},{32,160},{160,32},{48,176},{176,... | collective-permute-start | bytes 3145736 | tf_op jit(solution)/shard_map/cond/branch_1_fun/ppermute | solution.py:45
  247.8 1.9 collective-permute-start.10
  249.7 7.3 %collective-permute-start.11 = (bf16[128,512]{1,0:T(8,128)(2,1)}, bf16[128,512]{1,0:T(8,128)(2,1)S(1)}, u32[]{:S(2)}, u32[]{:S(2)}) collective-permute-start(bf16[128,512]{1,0:T(8,128)(2,1)} %get-tuple-element.455), channel_id=1, source_target_pairs={{0,128},{128,0},{16,144},{144,16},{32,160},{160,32},{48,176},{176,... | collective-permute-start | bytes 393224 | tf_op jit(solution)/shard_map/cond/branch_1_fun/ppermute | solution.py:45
  257.0 100.8 %collective-permute-done.10 = bf16[128,512]{1,0:T(8,128)(2,1)S(1)} collective-permute-done((bf16[128,512]{1,0:T(8,128)(2,1)}, bf16[128,512]{1,0:T(8,128)(2,1)S(1)}, u32[]{:S(2)}, u32[]{:S(2)}) %collective-permute-start.10) | collective-permute-done | bytes 131104 | tf_op jit(solution)/shard_map/cond/branch_1_fun/ppermute | solution.py:45
  358.4 2.2 collective-permute-done.11
  362.2 2.3 copy.329
  364.5 1.6 copy.330
  366.1 1.6 copy.331
  (524 shorter events, 40.4 us)
Async XLA Ops:
  0.6 14.8 %copy-start = (bf16[128,512]{1,0:T(8,128)(2,1)S(1)}, bf16[128,512]{1,0:T(8,128)(2,1)}, u32[]{:S(2)}) copy-start(bf16[128,512]{1,0:T(8,128)(2,1)} %param.81) | copy-start | bytes 393220
  0.6 12.8 %copy-start.1 = (bf16[128,4096]{1,0:T(8,128)(2,1)S(1)}, bf16[128,4096]{1,0:T(8,128)(2,1)}, u32[]{:S(2)}) copy-start(bf16[128,4096]{1,0:T(8,128)(2,1)} %param.83) | copy-start | bytes 3145732
  3.0 12.4 %copy-start.63 = (bf16[128,512]{1,0:T(8,128)(2,1)S(1)}, bf16[128,512]{1,0:T(8,128)(2,1)}, u32[]{:S(2)}) copy-start(bf16[128,512]{1,0:T(8,128)(2,1)} %param.82) | copy-start | bytes 393220
  3.0 22.0 %all-to-all-start.1 = ((bf16[128,16,256]{0,2,1:T(8,128)(2,1)}), bf16[128,16,256]{0,2,1:T(8,128)(2,1)S(1)}, u32[]{:S(2)}, u32[]{:S(2)}) async-start(bf16[128,16,256]{0,2,1:T(8,128)(2,1)} %bitcast.12), calls=%async_computation.1 | async-start | bytes 2097152 | tf_op jit(solution)/shard_map/all_to_all | solution.py:99
  10.7 54.6 %copy-start.96 = (s32[256]{0:T(256)}, s32[256]{0:T(256)S(1)}, u32[]{:S(2)}) copy-start(s32[256]{0:T(256)S(1)} %iota_add_fusion.14) | copy-start | bytes 3076
  11.9 51.9 %copy-start.128 = (s32[256]{0:T(256)}, s32[256]{0:T(256)S(1)}, u32[]{:S(2)}) copy-start(s32[256]{0:T(256)S(1)} %iota_add_fusion.11) | copy-start | bytes 3076
  11.9 48.8 %copy-start.125 = (s32[256]{0:T(256)}, s32[256]{0:T(256)S(1)}, u32[]{:S(2)}) copy-start(s32[256]{0:T(256)S(1)} %iota_add_fusion.10) | copy-start | bytes 3076
  11.9 45.7 %copy-start.122 = (s32[256]{0:T(256)}, s32[256]{0:T(256)S(1)}, u32[]{:S(2)}) copy-start(s32[256]{0:T(256)S(1)} %iota_add_fusion.9) | copy-start | bytes 3076
  11.9 42.5 %copy-start.119 = (s32[256]{0:T(256)}, s32[256]{0:T(256)S(1)}, u32[]{:S(2)}) copy-start(s32[256]{0:T(256)S(1)} %iota_add_fusion.8) | copy-start | bytes 3076
  15.4 48.4 %copy-start.87 = (s32[384]{0:T(512)}, s32[384]{0:T(512)S(1)}, u32[]{:S(2)}) copy-start(s32[384]{0:T(512)S(1)} %iota_add_fusion.4) | copy-start | bytes 4612
  15.4 45.3 %copy-start.78 = (s32[384]{0:T(512)}, s32[384]{0:T(512)S(1)}, u32[]{:S(2)}) copy-start(s32[384]{0:T(512)S(1)} %iota_add_fusion.3) | copy-start | bytes 4612
  25.0 20.3 %all-to-all-start = ((bf16[128,16,256]{2,0,1:T(8,128)(2,1)}), bf16[128,16,256]{2,0,1:T(8,128)(2,1)S(1)}, u32[]{:S(2)}, u32[]{:S(2)}) async-start(bf16[128,16,256]{2,0,1:T(8,128)(2,1)} %pad_maximum_fusion), calls=%async_computation | async-start | bytes 2097152 | tf_op jit(solution)/shard_map/all_to_all | solution.py:20
  30.4 20.9 %copy-start.131 = (s32[256]{0:T(256)}, s32[256]{0:T(256)S(1)}, u32[]{:S(2)}) copy-start(s32[256]{0:T(256)S(1)} %iota_add_fusion.7) | copy-start | bytes 3076
  30.4 27.2 %copy-start.84 = (s32[384]{0:T(512)}, s32[384]{0:T(512)S(1)}, u32[]{:S(2)}) copy-start(s32[384]{0:T(512)S(1)} %iota_add_fusion.2) | copy-start | bytes 4612
  30.4 24.0 %copy-start.81 = (s32[384]{0:T(512)}, s32[384]{0:T(512)S(1)}, u32[]{:S(2)}) copy-start(s32[384]{0:T(512)S(1)} %iota_add_fusion.1) | copy-start | bytes 4612
  30.4 20.9 %copy-start.75 = (s32[384]{0:T(512)}, s32[384]{0:T(512)S(1)}, u32[]{:S(2)}) copy-start(s32[384]{0:T(512)S(1)} %iota_add_fusion) | copy-start | bytes 4612
  31.1 20.2 %copy-start.98 = (s32[256]{0:T(256)}, s32[256]{0:T(256)S(1)}, u32[]{:S(2)}) copy-start(s32[256]{0:T(256)S(1)} %get-tuple-element.515) | copy-start | bytes 3076
  31.1 23.3 %copy-start.101 = (s32[256]{0:T(256)}, s32[256]{0:T(256)S(1)}, u32[]{:S(2)}) copy-start(s32[256]{0:T(256)S(1)} %get-tuple-element.516) | copy-start | bytes 3076
  31.2 26.4 %copy-start.104 = (s32[256]{0:T(256)}, s32[256]{0:T(256)S(1)}, u32[]{:S(2)}) copy-start(s32[256]{0:T(256)S(1)} %get-tuple-element.517) | copy-start | bytes 3076
  31.2 29.5 %copy-start.107 = (s32[256]{0:T(256)}, s32[256]{0:T(256)S(1)}, u32[]{:S(2)}) copy-start(s32[256]{0:T(256)S(1)} %get-tuple-element.518) | copy-start | bytes 3076
  31.2 32.6 %copy-start.110 = (s32[256]{0:T(256)}, s32[256]{0:T(256)S(1)}, u32[]{:S(2)}) copy-start(s32[256]{0:T(256)S(1)} %get-tuple-element.519) | copy-start | bytes 3076
  31.8 28.9 %copy-start.64 = (s32[384]{0:T(512)}, s32[384]{0:T(512)S(1)}, u32[]{:S(2)}) copy-start(s32[384]{0:T(512)S(1)} %get-tuple-element.511) | copy-start | bytes 4612
  31.8 32.0 %copy-start.67 = (s32[384]{0:T(512)}, s32[384]{0:T(512)S(1)}, u32[]{:S(2)}) copy-start(s32[384]{0:T(512)S(1)} %get-tuple-element.512) | copy-start | bytes 4612
  45.4 27.5 %copy-start.4 = (bf16[128,16,256]{2,0,1:T(8,128)(2,1)}, bf16[128,16,256]{2,0,1:T(8,128)(2,1)S(1)}, u32[]{:S(2)}) copy-start(bf16[128,16,256]{2,0,1:T(8,128)(2,1)S(1)} %all-to-all-done) | copy-start | bytes 3145732
  45.4 29.1 %all-to-all-start.2 = ((bf16[128,16,256]{0,2,1:T(8,128)(2,1)}), bf16[128,16,256]{0,2,1:T(8,128)(2,1)S(1)}, u32[]{:S(2)}, u32[]{:S(2)}) async-start(bf16[128,16,256]{0,2,1:T(8,128)(2,1)} %bitcast.20), calls=%async_computation.2 | async-start | bytes 2097152 | tf_op jit(solution)/shard_map/all_to_all | solution.py:100
  60.7 7.6 %copy-start.70 = (s32[384]{0:T(512)S(1)}, s32[384]{0:T(512)}, u32[]{:S(2)}) copy-start(s32[384]{0:T(512)} %get-tuple-element.513) | copy-start | bytes 4612
  60.7 7.6 %copy-start.93 = (s32[384]{0:T(512)S(1)}, s32[384]{0:T(512)}, u32[]{:S(2)}) copy-start(s32[384]{0:T(512)} %iota_add_fusion.5) | copy-start | bytes 4612
  60.7 7.6 %copy-start.113 = (s32[256]{0:T(256)S(1)}, s32[256]{0:T(256)}, u32[]{:S(2)}) copy-start(s32[256]{0:T(256)} %get-tuple-element.520) | copy-start | bytes 3076
  60.7 7.6 %copy-start.134 = (s32[256]{0:T(256)S(1)}, s32[256]{0:T(256)}, u32[]{:S(2)}) copy-start(s32[256]{0:T(256)} %iota_add_fusion.12) | copy-start | bytes 3076
  63.8 7.6 %copy-start.73 = (s32[384]{0:T(512)S(1)}, s32[384]{0:T(512)}, u32[]{:S(2)}) copy-start(s32[384]{0:T(512)} %get-tuple-element.514) | copy-start | bytes 4612
  63.8 7.6 %copy-start.90 = (s32[384]{0:T(512)S(1)}, s32[384]{0:T(512)}, u32[]{:S(2)}) copy-start(s32[384]{0:T(512)} %iota_add_fusion.6) | copy-start | bytes 4612
  63.8 7.6 %copy-start.116 = (s32[256]{0:T(256)S(1)}, s32[256]{0:T(256)}, u32[]{:S(2)}) copy-start(s32[256]{0:T(256)} %get-tuple-element.521) | copy-start | bytes 3076
  63.8 7.6 %copy-start.137 = (s32[256]{0:T(256)S(1)}, s32[256]{0:T(256)}, u32[]{:S(2)}) copy-start(s32[256]{0:T(256)} %iota_add_fusion.13) | copy-start | bytes 3076
  75.9 16.6 %copy-start.2 = (bf16[2048,2,128]{0,2,1:T(8,128)(2,1)}, bf16[2048,2,128]{0,2,1:T(8,128)(2,1)S(1)}, u32[]{:S(2)}) copy-start(bf16[2048,2,128]{0,2,1:T(8,128)(2,1)S(1)} %reshape.991) | copy-start | bytes 3145732
  75.9 4.1 %copy-start.46 = (f32[256,256]{0,1:T(8,128)S(1)}, f32[256,256]{0,1:T(8,128)}, u32[]{:S(2)}) copy-start(f32[256,256]{0,1:T(8,128)} %get-tuple-element.542) | copy-start | bytes 786436
  82.8 9.7 %copy-start.155 = (f32[256]{0:T(256)}, f32[256]{0:T(256)S(1)}, u32[]{:S(2)}) copy-start(f32[256]{0:T(256)S(1)} %fusion.119) | copy-start | bytes 3076
  83.0 8.1 %copy-start.161 = (f32[256]{0:T(256)}, f32[256]{0:T(256)S(1)}, u32[]{:S(2)}) copy-start(f32[256]{0:T(256)S(1)} %fusion.117) | copy-start | bytes 3076
  83.3 6.6 %copy-start.165 = (f32[256]{0:T(256)}, f32[256]{0:T(256)S(1)}, u32[]{:S(2)}) copy-start(f32[256]{0:T(256)S(1)} %fusion.115) | copy-start | bytes 3076
  83.5 5.0 %copy-start.171 = (f32[256]{0:T(256)}, f32[256]{0:T(256)S(1)}, u32[]{:S(2)}) copy-start(f32[256]{0:T(256)S(1)} %fusion.113) | copy-start | bytes 3076
  84.6 8.5 %copy-start.183 = (f32[256]{0:T(256)}, f32[256]{0:T(256)S(1)}, u32[]{:S(2)}) copy-start(f32[256]{0:T(256)S(1)} %get-tuple-element.505) | copy-start | bytes 3076
  85.9 8.1 %copy-start.185 = (f32[256]{0:T(256)}, f32[256]{0:T(256)S(1)}, u32[]{:S(2)}) copy-start(f32[256]{0:T(256)S(1)} %get-tuple-element.503) | copy-start | bytes 3076
  87.2 6.8 %copy-start.187 = (f32[256]{0:T(256)}, f32[256]{0:T(256)S(1)}, u32[]{:S(2)}) copy-start(f32[256]{0:T(256)S(1)} %get-tuple-element.501) | copy-start | bytes 3076
  88.5 6.4 %copy-start.189 = (f32[256]{0:T(256)}, f32[256]{0:T(256)S(1)}, u32[]{:S(2)}) copy-start(f32[256]{0:T(256)S(1)} %get-tuple-element.499) | copy-start | bytes 3076
  89.8 5.1 %copy-start.193 = (f32[256]{0:T(256)}, f32[256]{0:T(256)S(1)}, u32[]{:S(2)}) copy-start(f32[256]{0:T(256)S(1)} %get-tuple-element.497) | copy-start | bytes 3076
  91.1 4.8 %copy-start.191 = (f32[256]{0:T(256)}, f32[256]{0:T(256)S(1)}, u32[]{:S(2)}) copy-start(f32[256]{0:T(256)S(1)} %get-tuple-element.495) | copy-start | bytes 3076
  101.3 8.2 %copy-start.9 = (bf16[256,384]{0,1:T(8,128)(2,1)S(1)}, bf16[256,384]{0,1:T(8,128)(2,1)}, u32[]{:S(2)}) copy-start(bf16[256,384]{0,1:T(8,128)(2,1)} %copy-done.8) | copy-start | bytes 589828
  101.3 8.4 %copy-start.7 = (bf16[256,384]{0,1:T(8,128)(2,1)S(1)}, bf16[256,384]{0,1:T(8,128)(2,1)}, u32[]{:S(2)}) copy-start(bf16[256,384]{0,1:T(8,128)(2,1)} %copy-done.6) | copy-start | bytes 589828
  101.3 8.6 %copy-start.13 = (bf16[256,384]{0,1:T(8,128)(2,1)S(1)}, bf16[256,384]{0,1:T(8,128)(2,1)}, u32[]{:S(2)}) copy-start(bf16[256,384]{0,1:T(8,128)(2,1)} %copy-done.12) | copy-start | bytes 589828
  101.3 21.2 %all-to-all-start.3 = ((bf16[16,2,16384]{2,1,0:T(2,128)(2,1)}), bf16[16,2,16384]{2,1,0:T(2,128)(2,1)S(1)}, u32[]{:S(2)}, u32[]{:S(2)}) async-start(bf16[16,2,16384]{2,1,0:T(2,128)(2,1)} %reshape.1002), calls=%async_computation.3 | async-start | bytes 2097152 | tf_op jit(solution)/shard_map/all_to_all | solution.py:129
  119.1 8.8 %copy-start.148 = (f32[256]{0:T(256)S(1)}, f32[256]{0:T(256)}, u32[]{:S(2)}) copy-start(f32[256]{0:T(256)} %get-tuple-element.564) | copy-start | bytes 3076
  119.1 8.8 %copy-start.172 = (f32[256]{0:T(256)S(1)}, f32[256]{0:T(256)}, u32[]{:S(2)}) copy-start(f32[256]{0:T(256)} %copy-done.171) | copy-start | bytes 3076
  122.5 6.8 %copy-start.146 = (f32[256]{0:T(256)S(1)}, f32[256]{0:T(256)}, u32[]{:S(2)}) copy-start(f32[256]{0:T(256)} %get-tuple-element.570) | copy-start | bytes 3076
  122.5 6.8 %copy-start.166 = (f32[256]{0:T(256)S(1)}, f32[256]{0:T(256)}, u32[]{:S(2)}) copy-start(f32[256]{0:T(256)} %copy-done.165) | copy-start | bytes 3076
  122.5 20.0 %all-to-all-start.4 = ((f32[2048,1,128]{2,1,0:T(1,128)}), f32[2048,1,128]{2,1,0:T(1,128)}, u32[]{:S(2)}, u32[]{:S(2)}) async-start(f32[2048,1,128]{2,1,0:T(1,128)} %bitcast.105), calls=%async_computation.4 | async-start | bytes 2097152 | tf_op jit(solution)/shard_map/all_to_all | solution.py:135
  142.5 19.6 %all-to-all-start.5 = ((f32[2048,1,128]{2,1,0:T(1,128)}), f32[2048,1,128]{2,1,0:T(1,128)}, u32[]{:S(2)}, u32[]{:S(2)}) async-start(f32[2048,1,128]{2,1,0:T(1,128)} %bitcast.111), calls=%async_computation.5 | async-start | bytes 2097152 | tf_op jit(solution)/shard_map/all_to_all | solution.py:136
  164.1 11.2 %collective-permute-start = (bf16[128,4096]{1,0:T(8,128)(2,1)S(1)}, bf16[128,4096]{1,0:T(8,128)(2,1)}, u32[]{:S(2)}, u32[]{:S(2)}) collective-permute-start(bf16[128,4096]{1,0:T(8,128)(2,1)S(1)} %copy.244), channel_id=1, source_target_pairs={{0,16},{16,0},{32,48},{48,32},{64,80},{80,64},{96,112},{112,96},{1... | collective-permute-start | bytes 3145736 | tf_op jit(solution)/shard_map/cond/branch_1_fun/ppermute | solution.py:45
  169.7 4.5 %collective-permute-start.1 = (bf16[128,512]{1,0:T(8,128)(2,1)S(1)}, bf16[128,512]{1,0:T(8,128)(2,1)}, u32[]{:S(2)}, u32[]{:S(2)}) collective-permute-start(bf16[128,512]{1,0:T(8,128)(2,1)S(1)} %copy.245), channel_id=1, source_target_pairs={{0,16},{16,0},{32,48},{48,32},{64,80},{80,64},{96,112},{112,96},{1... | collective-permute-start | bytes 393224 | tf_op jit(solution)/shard_map/cond/branch_1_fun/ppermute | solution.py:45
  171.7 3.5 collective-permute-start.2
  175.3 62.8 %collective-permute-start.6 = (bf16[128,4096]{1,0:T(8,128)(2,1)}, bf16[128,4096]{1,0:T(8,128)(2,1)S(1)}, u32[]{:S(2)}, u32[]{:S(2)}) collective-permute-start(bf16[128,4096]{1,0:T(8,128)(2,1)} %get-tuple-element.450), channel_id=1, source_target_pairs={{0,64},{64,0},{16,80},{80,16},{32,96},{96,32},{48,112},{112,48},{1... | collective-permute-start | bytes 3145736 | tf_op jit(solution)/shard_map/cond/branch_1_fun/ppermute | solution.py:45
  180.3 54.3 %collective-permute-start.7 = (bf16[128,512]{1,0:T(8,128)(2,1)}, bf16[128,512]{1,0:T(8,128)(2,1)S(1)}, u32[]{:S(2)}, u32[]{:S(2)}) collective-permute-start(bf16[128,512]{1,0:T(8,128)(2,1)} %get-tuple-element.451), channel_id=1, source_target_pairs={{0,64},{64,0},{16,80},{80,16},{32,96},{96,32},{48,112},{112,48},{1... | collective-permute-start | bytes 393224 | tf_op jit(solution)/shard_map/cond/branch_1_fun/ppermute | solution.py:45
  182.2 55.1 %collective-permute-start.8 = (bf16[128,512]{1,0:T(8,128)(2,1)}, bf16[128,512]{1,0:T(8,128)(2,1)S(1)}, u32[]{:S(2)}, u32[]{:S(2)}) collective-permute-start(bf16[128,512]{1,0:T(8,128)(2,1)} %get-tuple-element.452), channel_id=1, source_target_pairs={{0,64},{64,0},{16,80},{80,16},{32,96},{96,32},{48,112},{112,48},{1... | collective-permute-start | bytes 393224 | tf_op jit(solution)/shard_map/cond/branch_1_fun/ppermute | solution.py:45
  239.0 122.3 %collective-permute-start.9 = (bf16[128,4096]{1,0:T(8,128)(2,1)}, bf16[128,4096]{1,0:T(8,128)(2,1)S(1)}, u32[]{:S(2)}, u32[]{:S(2)}) collective-permute-start(bf16[128,4096]{1,0:T(8,128)(2,1)} %get-tuple-element.453), channel_id=1, source_target_pairs={{0,128},{128,0},{16,144},{144,16},{32,160},{160,32},{48,176},{176,... | collective-permute-start | bytes 3145736 | tf_op jit(solution)/shard_map/cond/branch_1_fun/ppermute | solution.py:45
  247.8 110.0 %collective-permute-start.10 = (bf16[128,512]{1,0:T(8,128)(2,1)}, bf16[128,512]{1,0:T(8,128)(2,1)S(1)}, u32[]{:S(2)}, u32[]{:S(2)}) collective-permute-start(bf16[128,512]{1,0:T(8,128)(2,1)} %get-tuple-element.454), channel_id=1, source_target_pairs={{0,128},{128,0},{16,144},{144,16},{32,160},{160,32},{48,176},{176,... | collective-permute-start | bytes 393224 | tf_op jit(solution)/shard_map/cond/branch_1_fun/ppermute | solution.py:45
  249.7 110.9 %collective-permute-start.11 = (bf16[128,512]{1,0:T(8,128)(2,1)}, bf16[128,512]{1,0:T(8,128)(2,1)S(1)}, u32[]{:S(2)}, u32[]{:S(2)}) collective-permute-start(bf16[128,512]{1,0:T(8,128)(2,1)} %get-tuple-element.455), channel_id=1, source_target_pairs={{0,128},{128,0},{16,144},{144,16},{32,160},{160,32},{48,176},{176,... | collective-permute-start | bytes 393224 | tf_op jit(solution)/shard_map/cond/branch_1_fun/ppermute | solution.py:45
  (149 other events, 238.4 us)
where the time goes:
time: 369 us; the launch traced here: 368 us
  waiting for transfers between devices  197 us (53%)
  starting transfers between devices  73.6 us (20%)
  matrix products  49.2 us (13%)
  local copies, waits for them, and re-layouts  29.4 us (8%)
  other arithmetic  13.8 us (4%)
  between operations  4.38 us (1%)
    ppermute x9, waiting for transfers between devices, from_partner(): return lax.ppermute(block, axis, route)  154 us
    dot_general x80, matrix products, product(): lax.dot_general(left, right, dims, preferred_element_type=jnp.float32)  49.2 us
    ppermute x9, starting transfers between devices, from_partner(): return lax.ppermute(block, axis, route)  39 us
    unnamed x405, local copies, waits for them, and re-layouts  17.1 us
    all_to_all x1, waiting for transfers between devices, in_one_piece(): lax.all_to_all(both, axis, split_axis=split_dim, concat_axis=concat_dim,...  12.4 us
    all_to_all x1, waiting for transfers between devices, body(): lax.all_to_all(dv_stack, 'seq', split_axis=0, concat_axis=1, tiled=True)  10.5 us
    all_to_all x1, waiting for transfers between devices, body(): lax.all_to_all(dk_stack, 'seq', split_axis=0, concat_axis=1, tiled=True)  8.53 us
    all_to_all x1, waiting for transfers between devices, body(): lax.all_to_all(query_split, 'seq', split_axis=1, concat_axis=0, tiled=True)  8.23 us
  transfers between devices with their start and end apart: 15, of which 10 were waited for; matrix products, arithmetic and copies ran while one was open for 15% of the time, Pallas kernels for 0%

commit v1 on v0

v1 whole, which is shorter than its diff:
```python
import jax
import jax.numpy as jnp
from jax import lax
from jax.sharding import PartitionSpec as P

HQ = 32
KV = 4
DH = 128


def product(left, right, spec):
    return jnp.einsum(spec, left, right, preferred_element_type=jnp.float32)


def paired(block, axis, mask):
    count = lax.axis_size(axis)

    def route(m):
        return lambda x: lax.ppermute(x, axis, [(d, d ^ m) for d in range(count)])

    branches = [route(m) for m in range(1, count)]
    return lax.switch(mask - 1, branches, block)


def body(queries, keys, values, grad_out, doc_lengths, swap_mask):
    seq_count = lax.axis_size("seq")
    rows = queries.shape[0]
    group = HQ // KV
    scale = DH ** (-0.5)
    s = lax.axis_index("seq")
    dp = lax.axis_index("dp")

    kv_own = jnp.concatenate([keys, values], axis=1)
    kv_prev = lax.ppermute(kv_own, "seq", [(i, i + 1) for i in range(seq_count - 1)])
    key_band = jnp.concatenate([kv_prev[:, : KV * DH], keys], axis=0).reshape(2 * rows, KV, DH)
    value_band = jnp.concatenate([kv_prev[:, KV * DH :], values], axis=0).reshape(2 * rows, KV, DH)

    lengths = lax.dynamic_slice_in_dim(doc_lengths, dp, 1, 0)[0]
    ends = jnp.cumsum(lengths)
    q_pos = s * rows + jnp.arange(rows, dtype=jnp.int32)
    k_pos = s * rows - rows + jnp.arange(2 * rows, dtype=jnp.int32)
    seg_q = jnp.sum((ends[None, :] <= q_pos[:, None]).astype(jnp.int32), axis=1)
    seg_k = jnp.sum((ends[None, :] <= k_pos[:, None]).astype(jnp.int32), axis=1)
    allowed = (
        (k_pos[None, :] <= q_pos[:, None])
        & (k_pos[None, :] >= 0)
        & (seg_k[None, :] == seg_q[:, None])
    )
    allowed = allowed[None, :, None, :]

    q = queries.reshape(rows, KV, group, DH)
    do = grad_out.reshape(rows, KV, group, DH)
    scores = product(q, key_band, "tghd,sgd->gths")
    dprobs = product(do, value_band, "tghd,sgd->gths")
    scores = jnp.where(allowed, scores * scale, -1e30)
    peak = jnp.max(scores, axis=3, keepdims=True)
    expo = jnp.where(allowed, jnp.exp(scores - peak), 0.0)
    probs = expo / jnp.sum(expo, axis=3, keepdims=True)
    probs_low = probs.astype(jnp.bfloat16)
    delta = jnp.sum(probs * dprobs, axis=3, keepdims=True)
    dscores = (probs * (dprobs - delta)).astype(jnp.bfloat16)

    dq = (product(dscores, key_band, "gths,sgd->tghd") * scale).astype(jnp.bfloat16)
    dk_band = product(dscores, q, "gths,tghd->sgd") * scale
    dv_band = product(probs_low, do, "gths,tghd->sgd")

    back = jnp.concatenate(
        [dk_band[:rows].reshape(rows, KV * DH), dv_band[:rows].reshape(rows, KV * DH)], axis=1
    )
    back = lax.ppermute(back, "seq", [(i + 1, i) for i in range(seq_count - 1)])
    dk = (dk_band[rows:].reshape(rows, KV * DH) + back[:, : KV * DH]).astype(jnp.bfloat16)
    dv = (dv_band[rows:].reshape(rows, KV * DH) + back[:, KV * DH :]).astype(jnp.bfloat16)

    out = jnp.concatenate([dq.reshape(rows, HQ * DH), dk, dv], axis=1)
    out = paired(out, "dp", swap_mask[0])
    return out[:, : HQ * DH], out[:, HQ * DH : HQ * DH + KV * DH], out[:, HQ * DH + KV * DH :]


def solution(mesh):
    return jax.shard_map(
        body,
        mesh=mesh,
        in_specs=(
            P(("dp", "seq"), None),
            P(("dp", "seq"), None),
            P(("dp", "seq"), None),
            P(("dp", "seq"), None),
            P(),
            P(),
        ),
        out_specs=(P(("dp", "seq"), None), P(("dp", "seq"), None), P(("dp", "seq"), None)),
        check_vma=False,
    )
```

time: 369 us -> 176 us (0.48)
  waiting for transfers between devices: 197 us -> 119 us
  starting transfers between devices: 73.6 us -> 23.7 us
  matrix products: 49.2 us -> 12 us
  local copies, waits for them, and re-layouts: 29.4 us -> 14.1 us
  other arithmetic: 13.8 us -> 4.49 us
    all_to_all x6 -> x0, waiting for transfers between devices: 42.8 us -> none  [the longest x1 12.4 us: in_one_piece(): lax.all_to_all(both, axis, split_axis=split_dim, concat_axis=concat_dim,...]
    dot_general x80 -> x4, matrix products: 49.2 us -> 8.36 us  [product(): return jnp.einsum(spec, left, right, preferred_element_type=jnp.float32)]
    ppermute x9 -> x3, waiting for transfers between devices: 154 us -> 119 us  [the longest x1 111 us: route(): return lambda x: lax.ppermute(x, axis, [(d, d ^ m) for d in range(count)])]
    all_to_all x6 -> x0, starting transfers between devices: 34.6 us -> none  [the longest x1 7.7 us: body(): lax.all_to_all(query_split, 'seq', split_axis=1, concat_axis=0, tiled=True)]
    ppermute x9 -> x3, starting transfers between devices: 39 us -> 23.7 us  [the longest x1 17.7 us: route(): return lambda x: lax.ppermute(x, axis, [(d, d ^ m) for d in range(count)])]
    unnamed x405 -> x18, local copies, waits for them, and re-layouts: 17.1 us -> 2.51 us
    reduce_sum x11 -> x2, other arithmetic: 5.06 us -> 0.18 us  [the longest x1 0.09 us: body(): seg_k = jnp.sum((ends[None, :] <= k_pos[:, None]).astype(jnp.int32), axis=1)]
    cond x6 -> x0, local copies, waits for them, and re-layouts: 4.57 us -> none
  transfers between devices with their start and end apart: 15 -> 3, of which waited for: 10 -> 2; matrix products, arithmetic and copies ran while one was open for 15% -> 4% of each run, Pallas kernels for 0% -> 0%
where the time goes in v1:
time: 176 us; the launch traced here: 175 us
  waiting for transfers between devices  119 us (68%)
  starting transfers between devices  23.7 us (13%)
  local copies, waits for them, and re-layouts  14.1 us (8%)
  matrix products  12 us (7%)
  other arithmetic  4.49 us (3%)
    ppermute x1, waiting for transfers between devices, route(): return lambda x: lax.ppermute(x, axis, [(d, d ^ m) for d in range(count)])  111 us
    ppermute x1, starting transfers between devices, route(): return lambda x: lax.ppermute(x, axis, [(d, d ^ m) for d in range(count)])  17.7 us
    dot_general x4, matrix products, product(): return jnp.einsum(spec, left, right, preferred_element_type=jnp.float32)  8.36 us
    ppermute x1, waiting for transfers between devices, body(): back = lax.ppermute(back, 'seq', [(i + 1, i) for i in range(seq_count - 1)])  7.59 us
    ppermute x1, starting transfers between devices, body(): lax.ppermute(kv_own, 'seq', [(i, i + 1) for i in range(seq_count - 1)])  4.72 us
    sub x1, matrix products, body(): expo = jnp.where(allowed, jnp.exp(scores - peak), 0.0)  3.62 us
  transfers between devices with their start and end apart: 3, of which 2 were waited for; matrix products, arithmetic and copies ran while one was open for 4% of the time, Pallas kernels for 0%

profile of v1, /device:TPU:1, one launch (start us, length us, event | category | flops | bytes accessed | tf_op | source)
XLA Modules:
  0.0 174.9 jit_solution(2132605820281343349)
XLA Ops:
  0.6 0.0 copy-start
  0.6 0.0 copy-start.3
  0.7 1.1 copy.42
  1.8 1.0 copy.43
  2.8 0.7 pad_maximum_fusion.2
  3.5 4.7 %collective-permute-start.31 = (bf16[128,1024]{0,1:T(8,128)(2,1)}, bf16[128,1024]{0,1:T(8,128)(2,1)}, u32[]{:S(2)}, u32[]{:S(2)}) collective-permute-start(bf16[128,1024]{0,1:T(8,128)(2,1)} %pad_maximum_fusion.2), channel_id=1, source_target_pairs={{0,1},{1,2},{2,3},{3,4},{4,5},{5,6},{6,7},{7,8},{8,9},{9,10},{10,1... | collective-permute-start | bytes 786440 | tf_op jit(solution)/shard_map/ppermute | solution.py:34
  8.2 0.0 copy-done
  8.3 0.1 copy.45
  8.3 0.1 reduce-window.8
  8.4 0.1 reduce
  8.5 0.1 convert_reduce_fusion
  8.6 0.1 convert_reduce_fusion.1
  8.7 1.6 copy.73
  10.4 0.0 copy-done.3
  10.4 0.7 copy.74
  11.0 0.2 compare_and_fusion
  11.2 0.0 collective-permute-done.31
  11.2 1.0 fusion.24
  12.2 0.1 pad_maximum_fusion.3
  12.3 0.0 copy-start.6
  12.3 3.6 %fusion.25 = (f32[4,128,8]{1,2,0:T(8,128)S(1)}, f32[4,128,8,256]{1,3,2,0:T(8,128)}) fusion(pred[128,256]{0,1:T(8,128)(4,1)S(1)} %compare_and_fusion, bf16[256,4,128,1]{0,2,3,1:T(8,128)(2,1)S(1)} %bitcast.79, bf16[128,4,8,128]{0,3,2,1:T(8,128)(2,1)S(1)} %bitcast.70), kind=kOutput, calls=%fused_computation.43 | convolution fusion | flops 273678592 | bytes 5554176 | tf_op jit(solution)/shard_map/sub | solution.py:57
  15.9 0.0 copy-done.6
  15.9 3.0 %fusion.10 = f32[256,4,128]{0,2,1:T(8,128)S(1)} fusion(bf16[128,4,8,128]{0,3,2,1:T(8,128)(2,1)S(1)} %bitcast.73, f32[4,128,8,256]{1,3,2,0:T(8,128)} %get-tuple-element.77, f32[4,128,8]{1,2,0:T(8,128)S(1)} %get-tuple-element.76), kind=kOutput, calls=%fused_computation.18 | convolution fusion | flops 270532608 | bytes 5783552 | tf_op jit(solution)/shard_map/gths,tghd->sgd/dot_general | solution.py:12
  18.9 0.7 fusion.23
  19.7 0.8 copy.57
  20.5 0.0 copy-start.1
  20.5 3.1 %fusion.1 = (f32[4,128,8]{1,2,0:T(8,128)S(1)}, f32[4,256,128,8]{2,1,3,0:T(8,128)S(1)}) fusion(f32[4,128,8,256]{1,3,2,0:T(8,128)} %get-tuple-element.77, f32[4,128,8]{1,2,0:T(8,128)S(1)} %get-tuple-element.76, bf16[256,4,128,1]{0,2,3,1:T(8,128)(2,1)S(1)} %bitcast.81, bf16[128,4,8,128]{0,3,2,1:T(8,128)(2,1)S(1)} %bitcast.74), kind=kOutput, calls=%fused_computation.3 | convolution fusion | flops 271577088 | bytes 9732096 | tf_op jit(solution)/shard_map/tghd,sgd->gths/dot_general | solution.py:12
  23.6 0.3 copy-done.1
  24.0 1.1 fusion.3
  25.1 0.0 copy-start.5
  25.1 0.8 fusion.14
  25.9 0.0 copy-start.4
  26.0 0.1 copy.56
  26.1 0.0 copy-done.5
  26.1 0.0 copy-start.7
  26.1 0.9 pad_maximum_fusion.1
  27.0 1.3 collective-permute-start.32
  28.9 0.0 copy-done.4
  28.9 0.1 copy.59
  29.1 0.8 copy.58
  29.9 0.0 copy-done.7
  29.9 1.4 multiply_convert_fusion
  31.3 0.0 copy-start.2
  31.3 1.5 copy.60
  32.9 7.6 %collective-permute-done.32 = f32[128,1024]{1,0:T(8,128)} collective-permute-done((f32[128,1024]{1,0:T(8,128)}, f32[128,1024]{1,0:T(8,128)}, u32[]{:S(2)}, u32[]{:S(2)}) %collective-permute-start.32) | collective-permute-done | bytes 524320 | tf_op jit(solution)/shard_map/ppermute | solution.py:70
  40.5 0.0 copy-done.2
  40.5 1.1 fusion.18
  41.6 0.1 pad_maximum_fusion
  41.7 129.2 %conditional.1 = (bf16[128,5120]{1,0:T(8,128)(2,1)}) conditional(s32[]{:T(128)} %bitcast, bf16[128,5120]{1,0:T(8,128)(2,1)S(1)} %pad_maximum_fusion, bf16[128,5120]{1,0:T(8,128)(2,1)S(1)} %pad_maximum_fusion, bf16[128,5120]{1,0:T(8,128)(2,1)S(1)} %pad_maximum_fusion, ...), branch_computations={%region_6.7_spmd, %region_7.8_spmd, %region_8.9_spmd, %region_9.10... | conditional | bytes 5242928 | solution.py:22
  41.7 17.7 %collective-permute-start.24 = (bf16[128,5120]{1,0:T(8,128)(2,1)S(1)}, bf16[128,5120]{1,0:T(8,128)(2,1)}, u32[]{:S(2)}, u32[]{:S(2)}) collective-permute-start(bf16[128,5120]{1,0:T(8,128)(2,1)S(1)} %param.24), channel_id=1, source_target_pairs={{0,400},{16,384},{32,432},{48,416},{64,464},{80,448},{96,496},{112... | collective-permute-start | bytes 3932168 | tf_op jit(solution)/shard_map/cond/branch_24_fun/ppermute | solution.py:19
  59.5 111.4 %collective-permute-done.24 = bf16[128,5120]{1,0:T(8,128)(2,1)} collective-permute-done((bf16[128,5120]{1,0:T(8,128)(2,1)S(1)}, bf16[128,5120]{1,0:T(8,128)(2,1)}, u32[]{:S(2)}, u32[]{:S(2)}) %collective-permute-start.24) | collective-permute-done | bytes 1310752 | tf_op jit(solution)/shard_map/cond/branch_24_fun/ppermute | solution.py:19
  170.9 2.3 %slice.52 = bf16[128,4096]{1,0:T(8,128)(2,1)} slice(bf16[128,5120]{1,0:T(8,128)(2,1)} %get-tuple-element.82), slice={[0:128], [0:4096]} | slice | bytes 2097152 | tf_op jit(solution)/shard_map/slice | solution.py:76
  173.2 1.7 fusion.21
  (5 shorter events, 0.1 us)
Async XLA Ops:
  0.6 7.6 %copy-start = (s32[32,32]{1,0:T(8,128)S(1)}, s32[32,32]{1,0:T(8,128)}, u32[]{:S(2)}) copy-start(s32[32,32]{1,0:T(8,128)} %param.41) | copy-start | bytes 12292
  0.6 9.7 %copy-start.3 = (bf16[128,4096]{1,0:T(8,128)(2,1)S(1)}, bf16[128,4096]{1,0:T(8,128)(2,1)}, u32[]{:S(2)}) copy-start(bf16[128,4096]{1,0:T(8,128)(2,1)} %param.40) | copy-start | bytes 3145732
  3.5 7.7 %collective-permute-start.31 = (bf16[128,1024]{0,1:T(8,128)(2,1)}, bf16[128,1024]{0,1:T(8,128)(2,1)}, u32[]{:S(2)}, u32[]{:S(2)}) collective-permute-start(bf16[128,1024]{0,1:T(8,128)(2,1)} %pad_maximum_fusion.2), channel_id=1, source_target_pairs={{0,1},{1,2},{2,3},{3,4},{4,5},{5,6},{6,7},{7,8},{8,9},{9,10},{10,1... | collective-permute-start | bytes 786440 | tf_op jit(solution)/shard_map/ppermute | solution.py:34
  12.3 3.6 %copy-start.6 = (bf16[256,512]{0,1:T(8,128)(2,1)}, bf16[256,512]{0,1:T(8,128)(2,1)S(1)}, u32[]{:S(2)}) copy-start(bf16[256,512]{0,1:T(8,128)(2,1)S(1)} %get-tuple-element.80) | copy-start | bytes 786436
  20.5 3.4 %copy-start.1 = (f32[4,128,8,256]{1,3,2,0:T(8,128)S(1)}, f32[4,128,8,256]{1,3,2,0:T(8,128)}, u32[]{:S(2)}) copy-start(f32[4,128,8,256]{1,3,2,0:T(8,128)} %get-tuple-element.77) | copy-start | bytes 12582916
  25.1 1.0 copy-start.5
  25.9 3.0 %copy-start.4 = (f32[128,4,128]{0,2,1:T(8,128)S(1)}, f32[128,4,128]{0,2,1:T(8,128)}, u32[]{:S(2)}) copy-start(f32[128,4,128]{0,2,1:T(8,128)} %get-tuple-element.73) | copy-start | bytes 786436
  26.1 3.8 %copy-start.7 = (bf16[256,512]{0,1:T(8,128)(2,1)S(1)}, bf16[256,512]{0,1:T(8,128)(2,1)}, u32[]{:S(2)}) copy-start(bf16[256,512]{0,1:T(8,128)(2,1)} %copy-done.6) | copy-start | bytes 786436
  27.0 13.5 %collective-permute-start.32 = (f32[128,1024]{1,0:T(8,128)}, f32[128,1024]{1,0:T(8,128)}, u32[]{:S(2)}, u32[]{:S(2)}) collective-permute-start(f32[128,1024]{1,0:T(8,128)} %pad_maximum_fusion.1), channel_id=1, source_target_pairs={{1,0},{2,1},{3,2},{4,3},{5,4},{6,5},{7,6},{8,7},{9,8},{10,9},{11,1... | collective-permute-start | bytes 1572872 | tf_op jit(solution)/shard_map/ppermute | solution.py:70
  31.3 9.1 %copy-start.2 = (f32[128,512]{1,0:T(8,128)S(1)}, f32[128,512]{1,0:T(8,128)}, u32[]{:S(2)}) copy-start(f32[128,512]{1,0:T(8,128)} %copy.58) | copy-start | bytes 786436
  41.7 129.2 %collective-permute-start.24 = (bf16[128,5120]{1,0:T(8,128)(2,1)S(1)}, bf16[128,5120]{1,0:T(8,128)(2,1)}, u32[]{:S(2)}, u32[]{:S(2)}) collective-permute-start(bf16[128,5120]{1,0:T(8,128)(2,1)S(1)} %param.24), channel_id=1, source_target_pairs={{0,400},{16,384},{32,432},{48,416},{64,464},{80,448},{96,496},{112... | collective-permute-start | bytes 3932168 | tf_op jit(solution)/shard_map/cond/branch_24_fun/ppermute | solution.py:19

commit v2 on v1

v2 whole, which is shorter than its diff:
```python
import functools

import jax
import jax.numpy as jnp
from jax import lax
from jax.experimental import pallas as pl
from jax.experimental.pallas import tpu as pltpu
from jax.sharding import PartitionSpec as P

HQ = 32
KV = 4
DH = 128
INTERPRET = False

contract_last = (((1,), (1,)), ((), ()))
contract_inner = (((1,), (0,)), ((), ()))
contract_first = (((0,), (0,)), ((), ()))


def product(left, right, dims):
    return lax.dot_general(left, right, dims, preferred_element_type=jnp.float32)


def group_kernel(q_ref, do_ref, k_ref, v_ref, mask_ref, dq_ref, dk_ref, dv_ref):
    scale = DH ** (-0.5)
    group = HQ // KV
    key_band = k_ref[...]
    value_band = v_ref[...]
    allowed = mask_ref[...] != 0
    dk_acc = jnp.zeros(dk_ref.shape, jnp.float32)
    dv_acc = jnp.zeros(dv_ref.shape, jnp.float32)
    for h in range(group):
        cols = slice(h * DH, (h + 1) * DH)
        q = q_ref[:, cols]
        do = do_ref[:, cols]
        scores = product(q, key_band, contract_last)
        dprobs = product(do, value_band, contract_last)
        scores = jnp.where(allowed, scores * scale, -1e30)
        peak = jnp.max(scores, axis=1, keepdims=True)
        expo = jnp.where(allowed, jnp.exp(scores - peak), 0.0)
        probs = expo / jnp.sum(expo, axis=1, keepdims=True)
        delta = jnp.sum(probs * dprobs, axis=1, keepdims=True)
        dscores = (probs * (dprobs - delta)).astype(jnp.bfloat16)
        dq_ref[:, cols] = (product(dscores, key_band, contract_inner) * scale).astype(jnp.bfloat16)
        dk_acc = dk_acc + product(dscores, q, contract_first)
        dv_acc = dv_acc + product(probs.astype(jnp.bfloat16), do, contract_first)
    dk_ref[...] = dk_acc * scale
    dv_ref[...] = dv_acc


def attention_grads(queries, grad_out, key_band, value_band, mask):
    rows = queries.shape[0]
    band = key_band.shape[0]
    width = (HQ // KV) * DH
    wide = pl.BlockSpec((rows, width), lambda g: (0, g))
    narrow = pl.BlockSpec((band, DH), lambda g: (0, g))
    return pl.pallas_call(
        group_kernel,
        grid=(KV,),
        in_specs=[wide, wide, narrow, narrow, pl.BlockSpec((rows, band), lambda g: (0, 0))],
        out_specs=[wide, narrow, narrow],
        out_shape=[
            jax.ShapeDtypeStruct((rows, HQ * DH), jnp.bfloat16),
            jax.ShapeDtypeStruct((band, KV * DH), jnp.float32),
            jax.ShapeDtypeStruct((band, KV * DH), jnp.float32),
        ],
        interpret=INTERPRET,
    )(queries, grad_out, key_band, value_band, mask)


def paired(blocks, axis, mask):
    count = lax.axis_size(axis)

    def route(m):
        pairs = [(d, d ^ m) for d in range(count)]
        return lambda xs: tuple(lax.ppermute(x, axis, pairs) for x in xs)

    return lax.switch(mask - 1, [route(m) for m in range(1, count)], blocks)


def body(queries, keys, values, grad_out, doc_lengths, swap_mask):
    seq_count = lax.axis_size("seq")
    rows = queries.shape[0]
    s = lax.axis_index("seq")
    dp = lax.axis_index("dp")

    kv_own = jnp.concatenate([keys, values], axis=1)
    kv_prev = lax.ppermute(kv_own, "seq", [(i, i + 1) for i in range(seq_count - 1)])
    key_band = jnp.concatenate([kv_prev[:, : KV * DH], keys], axis=0)
    value_band = jnp.concatenate([kv_prev[:, KV * DH :], values], axis=0)

    lengths = lax.dynamic_slice_in_dim(doc_lengths, dp, 1, 0)[0]
    ends = jnp.cumsum(lengths)
    q_pos = s * rows + jnp.arange(rows, dtype=jnp.int32)
    k_pos = s * rows - rows + jnp.arange(2 * rows, dtype=jnp.int32)
    seg_q = jnp.sum((ends[None, :] <= q_pos[:, None]).astype(jnp.int32), axis=1)
    seg_k = jnp.sum((ends[None, :] <= k_pos[:, None]).astype(jnp.int32), axis=1)
    allowed = (
        (k_pos[None, :] <= q_pos[:, None])
        & (k_pos[None, :] >= 0)
        & (seg_k[None, :] == seg_q[:, None])
    )

    dq, dk_band, dv_band = attention_grads(queries, grad_out, key_band, value_band, allowed.astype(jnp.int32))

    back = jnp.concatenate([dk_band[:rows], dv_band[:rows]], axis=1)
    back = lax.ppermute(back, "seq", [(i + 1, i) for i in range(seq_count - 1)])
    dk = (dk_band[rows:] + back[:, : KV * DH]).astype(jnp.bfloat16)
    dv = (dv_band[rows:] + back[:, KV * DH :]).astype(jnp.bfloat16)
    return paired((dq, dk, dv), "dp", swap_mask[0])


def solution(mesh):
    return jax.shard_map(
        body,
        mesh=mesh,
        in_specs=(
            P(("dp", "seq"), None),
            P(("dp", "seq"), None),
            P(("dp", "seq"), None),
            P(("dp", "seq"), None),
            P(),
            P(),
        ),
        out_specs=(P(("dp", "seq"), None), P(("dp", "seq"), None), P(("dp", "seq"), None)),
        check_vma=False,
    )
```

time: 176 us -> 173 us (0.983)
  the two profiles are of different devices: /device:TPU:1 before, /device:TPU:39 now
where the time goes in v2:
time: 173 us
  waiting for transfers between devices  121 us (70%)
  starting transfers between devices  24.4 us (14%)
  Pallas kernels  16.2 us (9%)
  local copies, waits for them, and re-layouts  6.7 us (4%)
  other arithmetic  3.08 us (2%)
    ppermute x3, waiting for transfers between devices, route(): return lambda xs: tuple((lax.ppermute(x, axis, pairs) for x in xs))  104 us
    ppermute x3, starting transfers between devices, route(): return lambda xs: tuple((lax.ppermute(x, axis, pairs) for x in xs))  18.3 us
    pallas_call x1, Pallas kernels, attention_grads(): pl.pallas_call(group_kernel, grid=(KV,), in_specs=[wide, wide, narrow, na...  16.2 us
    ppermute x1, waiting for transfers between devices, body(): back = lax.ppermute(back, 'seq', [(i + 1, i) for i in range(seq_count - 1)])  10.4 us
    ppermute x1, waiting for transfers between devices, body(): lax.ppermute(kv_own, 'seq', [(i, i + 1) for i in range(seq_count - 1)])  6.7 us
    unnamed x13, local copies, waits for them, and re-layouts  5.54 us
  transfers between devices with their start and end apart: 5, of which 4 were waited for; matrix products, arithmetic and copies ran while one was open for 1% of the time, Pallas kernels for 0%

profile of v2, /device:TPU:39, one launch (start us, length us, event | category | flops | bytes accessed | tf_op | source)
XLA Modules:
  0.0 172.7 jit_solution(2969613294766338771)
XLA Ops:
  0.6 0.0 copy-start
  0.6 1.0 pad_maximum_fusion.1
  1.6 3.2 %collective-permute-start.93 = (bf16[128,1024]{1,0:T(8,128)(2,1)S(1)}, bf16[128,1024]{1,0:T(8,128)(2,1)S(1)}, u32[]{:S(2)}, u32[]{:S(2)}) collective-permute-start(bf16[128,1024]{1,0:T(8,128)(2,1)S(1)} %pad_maximum_fusion.1), channel_id=1, source_target_pairs={{0,1},{1,2},{2,3},{3,4},{4,5},{5,6},{6,7},{7,8},{8,9},{9,10},{10,1... | collective-permute-start | bytes 786440 | tf_op jit(solution)/shard_map/ppermute | solution.py:88
  4.9 0.0 copy-done
  4.9 0.1 copy.104
  5.0 0.1 reduce-window.8
  5.1 0.1 reduce
  5.2 0.1 convert_reduce_fusion.1
  5.3 0.1 convert_reduce_fusion
  5.4 0.8 and_convert_fusion.mask_ref
  6.1 0.0 copy-start.3
  6.1 0.0 copy-start.4
  6.1 6.7 %collective-permute-done.93 = bf16[128,1024]{1,0:T(8,128)(2,1)S(1)} collective-permute-done((bf16[128,1024]{1,0:T(8,128)(2,1)S(1)}, bf16[128,1024]{1,0:T(8,128)(2,1)S(1)}, u32[]{:S(2)}, u32[]{:S(2)}) %collective-permute-start.93) | collective-permute-done | bytes 262176 | tf_op jit(solution)/shard_map/ppermute | solution.py:88
  12.9 0.0 copy-done.3
  12.9 0.0 copy-done.4
  12.9 0.8 pad_maximum_fusion.2
  13.7 16.2 %shard_map.178 = (bf16[128,4096]{1,0:T(8,128)(2,1)S(1)}, f32[256,512]{1,0:T(8,128)}, f32[256,512]{1,0:T(8,128)}) custom-call(bf16[128,4096]{1,0:T(8,128)(2,1)} %q_ref.1, bf16[128,4096]{1,0:T(8,128)(2,1)} %do_ref.1, bf16[256,512]{1,0:T(8,128)(2,1)} %get-tuple-element.295.k_ref, bf16[256,512]{1,0:T(8,128)(2,1)} %get-tuple-element.296.v_ref, ...), custom_call_target="tpu_custom_call" | custom-call | tf_op jit(solution)/shard_map/pallas_call | solution.py:57
  29.9 0.0 copy-start.2
  29.9 1.0 slice.27
  30.9 0.1 copy-done.2
  31.0 0.0 copy-start.1
  31.1 2.9 %collective-permute-start.94 = (f32[128,1024]{1,0:T(8,128)S(1)}, f32[128,1024]{1,0:T(8,128)S(1)}, u32[]{:S(2)}, u32[]{:S(2)}) collective-permute-start(f32[128,1024]{1,0:T(8,128)S(1)} %pad_maximum_fusion), channel_id=1, source_target_pairs={{1,0},{2,1},{3,2},{4,3},{5,4},{6,5},{7,6},{8,7},{9,8},{10,9},{11,1... | collective-permute-start | bytes 1572872 | tf_op jit(solution)/shard_map/ppermute | solution.py:107
  34.7 10.4 %collective-permute-done.94 = f32[128,1024]{1,0:T(8,128)S(1)} collective-permute-done((f32[128,1024]{1,0:T(8,128)S(1)}, f32[128,1024]{1,0:T(8,128)S(1)}, u32[]{:S(2)}, u32[]{:S(2)}) %collective-permute-start.94) | collective-permute-done | bytes 524320 | tf_op jit(solution)/shard_map/ppermute | solution.py:107
  45.1 0.0 copy-done.1
  45.1 0.1 fusion
  45.2 122.1 %conditional.1 = (bf16[128,4096]{1,0:T(8,128)(2,1)}, bf16[128,512]{1,0:T(8,128)(2,1)}, bf16[128,512]{1,0:T(8,128)(2,1)}) conditional(s32[]{:T(128)} %bitcast, (bf16[128,4096]{1,0:T(8,128)(2,1)S(1)}, bf16[128,512]{1,0:T(8,128)(2,1)S(1)}, bf16[128,512]{1,0:T(8,128)(2,1)S(1)}) %tuple.131, ...), branch_computations={%region_3.4_spmd, %region_4.5_spmd, %region_5.6_spmd, %region_6.7_... | conditional | bytes 5243024 | solution.py:78
  45.2 9.7 %collective-permute-start.30 = (bf16[128,4096]{1,0:T(8,128)(2,1)S(1)}, bf16[128,4096]{1,0:T(8,128)(2,1)}, u32[]{:S(2)}, u32[]{:S(2)}) collective-permute-start(bf16[128,4096]{1,0:T(8,128)(2,1)S(1)} %get-tuple-element.216), channel_id=1, source_target_pairs={{0,176},{16,160},{32,144},{48,128},{64,240},{80,224},{96,208},{112... | collective-permute-start | bytes 3145736 | tf_op jit(solution)/shard_map/cond/branch_10_fun/ppermute | solution.py:76
  54.9 1.9 %collective-permute-start.31 = (bf16[128,512]{1,0:T(8,128)(2,1)S(1)}, bf16[128,512]{1,0:T(8,128)(2,1)}, u32[]{:S(2)}, u32[]{:S(2)}) collective-permute-start(bf16[128,512]{1,0:T(8,128)(2,1)S(1)} %get-tuple-element.217), channel_id=1, source_target_pairs={{0,176},{16,160},{32,144},{48,128},{64,240},{80,224},{96,208},{112... | collective-permute-start | bytes 393224 | tf_op jit(solution)/shard_map/cond/branch_10_fun/ppermute | solution.py:76
  56.9 6.7 %collective-permute-start.32 = (bf16[128,512]{1,0:T(8,128)(2,1)S(1)}, bf16[128,512]{1,0:T(8,128)(2,1)}, u32[]{:S(2)}, u32[]{:S(2)}) collective-permute-start(bf16[128,512]{1,0:T(8,128)(2,1)S(1)} %get-tuple-element.218), channel_id=1, source_target_pairs={{0,176},{16,160},{32,144},{48,128},{64,240},{80,224},{96,208},{112... | collective-permute-start | bytes 393224 | tf_op jit(solution)/shard_map/cond/branch_10_fun/ppermute | solution.py:76
  63.5 101.7 %collective-permute-done.31 = bf16[128,512]{1,0:T(8,128)(2,1)} collective-permute-done((bf16[128,512]{1,0:T(8,128)(2,1)S(1)}, bf16[128,512]{1,0:T(8,128)(2,1)}, u32[]{:S(2)}, u32[]{:S(2)}) %collective-permute-start.31) | collective-permute-done | bytes 131104 | tf_op jit(solution)/shard_map/cond/branch_10_fun/ppermute | solution.py:76
  165.3 2.0 %collective-permute-done.32 = bf16[128,512]{1,0:T(8,128)(2,1)} collective-permute-done((bf16[128,512]{1,0:T(8,128)(2,1)S(1)}, bf16[128,512]{1,0:T(8,128)(2,1)}, u32[]{:S(2)}, u32[]{:S(2)}) %collective-permute-start.32) | collective-permute-done | bytes 131104 | tf_op jit(solution)/shard_map/cond/branch_10_fun/ppermute | solution.py:76
  167.2 0.0 collective-permute-done.30
  167.2 2.3 %copy.202 = bf16[128,4096]{1,0:T(8,128)(2,1)} copy(bf16[128,4096]{1,0:T(8,128)(2,1)} %get-tuple-element.393) | data formatting | bytes 2097152
  169.5 1.6 copy.203
  171.1 1.6 copy.204
  (7 shorter events, 0.1 us)
Async XLA Ops:
  0.6 4.3 %copy-start = (s32[32,32]{1,0:T(8,128)S(1)}, s32[32,32]{1,0:T(8,128)}, u32[]{:S(2)}) copy-start(s32[32,32]{1,0:T(8,128)} %param.41) | copy-start | bytes 12292
  1.6 11.2 %collective-permute-start.93 = (bf16[128,1024]{1,0:T(8,128)(2,1)S(1)}, bf16[128,1024]{1,0:T(8,128)(2,1)S(1)}, u32[]{:S(2)}, u32[]{:S(2)}) collective-permute-start(bf16[128,1024]{1,0:T(8,128)(2,1)S(1)} %pad_maximum_fusion.1), channel_id=1, source_target_pairs={{0,1},{1,2},{2,3},{3,4},{4,5},{5,6},{6,7},{7,8},{8,9},{9,10},{10,1... | collective-permute-start | bytes 786440 | tf_op jit(solution)/shard_map/ppermute | solution.py:88
  6.1 6.7 %copy-start.3 = (bf16[128,512]{1,0:T(8,128)(2,1)S(1)}, bf16[128,512]{1,0:T(8,128)(2,1)}, u32[]{:S(2)}) copy-start(bf16[128,512]{1,0:T(8,128)(2,1)} %param.38) | copy-start | bytes 393220
  6.1 6.7 %copy-start.4 = (bf16[128,512]{1,0:T(8,128)(2,1)S(1)}, bf16[128,512]{1,0:T(8,128)(2,1)}, u32[]{:S(2)}) copy-start(bf16[128,512]{1,0:T(8,128)(2,1)} %param.39) | copy-start | bytes 393220
  29.9 1.1 copy-start.2
  31.0 14.0 %copy-start.1 = (f32[256,512]{1,0:T(8,128)S(1)}, f32[256,512]{1,0:T(8,128)}, u32[]{:S(2)}) copy-start(f32[256,512]{1,0:T(8,128)} %get-tuple-element.286) | copy-start | bytes 1572868
  31.1 14.0 %collective-permute-start.94 = (f32[128,1024]{1,0:T(8,128)S(1)}, f32[128,1024]{1,0:T(8,128)S(1)}, u32[]{:S(2)}, u32[]{:S(2)}) collective-permute-start(f32[128,1024]{1,0:T(8,128)S(1)} %pad_maximum_fusion), channel_id=1, source_target_pairs={{1,0},{2,1},{3,2},{4,3},{5,4},{6,5},{7,6},{8,7},{9,8},{10,9},{11,1... | collective-permute-start | bytes 1572872 | tf_op jit(solution)/shard_map/ppermute | solution.py:107
  45.2 122.1 %collective-permute-start.30 = (bf16[128,4096]{1,0:T(8,128)(2,1)S(1)}, bf16[128,4096]{1,0:T(8,128)(2,1)}, u32[]{:S(2)}, u32[]{:S(2)}) collective-permute-start(bf16[128,4096]{1,0:T(8,128)(2,1)S(1)} %get-tuple-element.216), channel_id=1, source_target_pairs={{0,176},{16,160},{32,144},{48,128},{64,240},{80,224},{96,208},{112... | collective-permute-start | bytes 3145736 | tf_op jit(solution)/shard_map/cond/branch_10_fun/ppermute | solution.py:76
  54.9 110.3 %collective-permute-start.31 = (bf16[128,512]{1,0:T(8,128)(2,1)S(1)}, bf16[128,512]{1,0:T(8,128)(2,1)}, u32[]{:S(2)}, u32[]{:S(2)}) collective-permute-start(bf16[128,512]{1,0:T(8,128)(2,1)S(1)} %get-tuple-element.217), channel_id=1, source_target_pairs={{0,176},{16,160},{32,144},{48,128},{64,240},{80,224},{96,208},{112... | collective-permute-start | bytes 393224 | tf_op jit(solution)/shard_map/cond/branch_10_fun/ppermute | solution.py:76
  56.9 110.4 %collective-permute-start.32 = (bf16[128,512]{1,0:T(8,128)(2,1)S(1)}, bf16[128,512]{1,0:T(8,128)(2,1)}, u32[]{:S(2)}, u32[]{:S(2)}) collective-permute-start(bf16[128,512]{1,0:T(8,128)(2,1)S(1)} %get-tuple-element.218), channel_id=1, source_target_pairs={{0,176},{16,160},{32,144},{48,128},{64,240},{80,224},{96,208},{112... | collective-permute-start | bytes 393224 | tf_op jit(solution)/shard_map/cond/branch_10_fun/ppermute | solution.py:76

commit v3 on v2

--- a/solution.py
+++ b/solution.py
@@ -1,5 +1,3 @@
-import functools
-
 import jax
 import jax.numpy as jnp
 from jax import lax
@@ -38,7 +36,7 @@
         scores = jnp.where(allowed, scores * scale, -1e30)
         peak = jnp.max(scores, axis=1, keepdims=True)
         expo = jnp.where(allowed, jnp.exp(scores - peak), 0.0)
-        probs = expo / jnp.sum(expo, axis=1, keepdims=True)
+        probs = expo * (1.0 / jnp.sum(expo, axis=1, keepdims=True))
         delta = jnp.sum(probs * dprobs, axis=1, keepdims=True)
         dscores = (probs * (dprobs - delta)).astype(jnp.bfloat16)
         dq_ref[:, cols] = (product(dscores, key_band, contract_inner) * scale).astype(jnp.bfloat16)
@@ -68,14 +66,26 @@
     )(queries, grad_out, key_band, value_band, mask)
 
 
-def paired(blocks, axis, mask):
-    count = lax.axis_size(axis)
+def paired(dq, dk_band, dv_band, mask):
+    dp_count = lax.axis_size("dp")
+    seq_count = lax.axis_size("seq")
+    rows = dq.shape[0]
 
     def route(m):
-        pairs = [(d, d ^ m) for d in range(count)]
-        return lambda xs: tuple(lax.ppermute(x, axis, pairs) for x in xs)
+        pairs = [(d, d ^ m) for d in range(dp_count)]
 
-    return lax.switch(mask - 1, [route(m) for m in range(1, count)], blocks)
+        def run(ops):
+            dq, dk_band, dv_band = ops
+            dq = lax.ppermute(dq, "dp", pairs)
+            back = jnp.concatenate([dk_band[:rows], dv_band[:rows]], axis=1)
+            back = lax.ppermute(back, "seq", [(i + 1, i) for i in range(seq_count - 1)])
+            own = jnp.concatenate([dk_band[rows:], dv_band[rows:]], axis=1)
+            dkv = lax.ppermute((own + back).astype(jnp.bfloat16), "dp", pairs)
+            return dq, dkv[:, : KV * DH], dkv[:, KV * DH :]
+
+        return run
+
+    return lax.switch(mask - 1, [route(m) for m in range(1, dp_count)], (dq, dk_band, dv_band))
 
 
 def body(queries, keys, values, grad_out, doc_lengths, swap_mask):
@@ -102,12 +112,7 @@
     )
 
     dq, dk_band, dv_band = attention_grads(queries, grad_out, key_band, value_band, allowed.astype(jnp.int32))
-
-    back = jnp.concatenate([dk_band[:rows], dv_band[:rows]], axis=1)
-    back = lax.ppermute(back, "seq", [(i + 1, i) for i in range(seq_count - 1)])
-    dk = (dk_band[rows:] + back[:, : KV * DH]).astype(jnp.bfloat16)
-    dv = (dv_band[rows:] + back[:, KV * DH :]).astype(jnp.bfloat16)
-    return paired((dq, dk, dv), "dp", swap_mask[0])
+    return paired(dq, dk_band, dv_band, swap_mask[0])
 
 
 def solution(mesh):

time: 173 us -> 68 us (0.39)
  the two profiles are of different devices: /device:TPU:39 before, /device:TPU:70 now
where the time goes in v3:
time: 68 us; the launch traced here: 67.7 us
  waiting for transfers between devices  30.4 us (45%)
  Pallas kernels  15.5 us (23%)
  starting transfers between devices  14.2 us (21%)
  other arithmetic  3.04 us (4%)
  local copies, waits for them, and re-layouts  2.63 us (4%)
  between operations  1.59 us (2%)
    ppermute x1, waiting for transfers between devices, run(): dkv = lax.ppermute((own + back).astype(jnp.bfloat16), 'dp', pairs)  16 us
    pallas_call x1, Pallas kernels, attention_grads(): pl.pallas_call(group_kernel, grid=(KV,), in_specs=[wide, wide, narrow, na...  15.5 us
    ppermute x1, waiting for transfers between devices, run(): back = lax.ppermute(back, 'seq', [(i + 1, i) for i in range(seq_count - 1)])  7.78 us
    ppermute x1, waiting for transfers between devices, body(): lax.ppermute(kv_own, 'seq', [(i, i + 1) for i in range(seq_count - 1)])  6.62 us
    ppermute x1, starting transfers between devices, run(): dq = lax.ppermute(dq, 'dp', pairs)  3.83 us
    ppermute x1, starting transfers between devices, run(): dkv = lax.ppermute((own + back).astype(jnp.bfloat16), 'dp', pairs)  3.82 us
    ppermute x1, starting transfers between devices, body(): lax.ppermute(kv_own, 'seq', [(i, i + 1) for i in range(seq_count - 1)])  3.48 us
    ppermute x1, starting transfers between devices, run(): back = lax.ppermute(back, 'seq', [(i + 1, i) for i in range(seq_count - 1)])  3.08 us
  transfers between devices with their start and end apart: 4, of which 3 were waited for; matrix products, arithmetic and copies ran while one was open for 2% of the time, Pallas kernels for 0%

profile of v3, /device:TPU:70, one launch (start us, length us, event | category | flops | bytes accessed | tf_op | source)
XLA Modules:
  0.0 67.7 jit_solution(7990366705466751341)
XLA Ops:
  0.6 0.0 copy-start
  0.6 1.0 %pad_maximum_fusion.31 = bf16[128,1024]{1,0:T(8,128)(2,1)S(1)} fusion(bf16[128,512]{1,0:T(8,128)(2,1)} %param.39, bf16[128,512]{1,0:T(8,128)(2,1)} %param.38), kind=kLoop, calls=%fused_computation.93 | loop fusion | flops 524288 | bytes 524288 | tf_op jit(solution)/shard_map/concatenate | solution.py:97
  1.6 3.5 %collective-permute-start.93 = (bf16[128,1024]{1,0:T(8,128)(2,1)S(1)}, bf16[128,1024]{1,0:T(8,128)(2,1)S(1)}, u32[]{:S(2)}, u32[]{:S(2)}) collective-permute-start(bf16[128,1024]{1,0:T(8,128)(2,1)S(1)} %pad_maximum_fusion.31), channel_id=1, source_target_pairs={{0,1},{1,2},{2,3},{3,4},{4,5},{5,6},{6,7},{7,8},{8,9},{9,10},{10,1... | collective-permute-start | bytes 786440 | tf_op jit(solution)/shard_map/ppermute | solution.py:98
  5.2 0.0 copy-done
  5.2 0.1 copy.104
  5.3 0.1 reduce-window.8
  5.3 0.1 reduce
  5.5 0.1 convert_reduce_fusion.1
  5.6 0.1 convert_reduce_fusion
  6.3 0.8 %and_convert_fusion.mask_ref = s32[128,256]{1,0:T(8,128)} fusion(s32[256]{0:T(256)S(1)} %convert_reduce_fusion, s32[256]{0:T(256)S(1)} %iota_add_fusion, s32[128]{0:T(128)S(1)} %convert_reduce_fusion.1, s32[128]{0:T(128)S(1)} %iota_add_fusion.1, pred[256]{0:T(512)(128)(4,1)S(1)} %broadcast_compare_fusion), kind=kLoop, calls=%fused_computation.96 | loop fusion | flops 163840 | bytes 134400 | tf_op jit(solution)/shard_map/convert_element_type | solution.py:114
  7.1 0.0 copy-start.2
  7.1 0.0 copy-start.3
  7.1 6.6 %collective-permute-done.93 = bf16[128,1024]{1,0:T(8,128)(2,1)S(1)} collective-permute-done((bf16[128,1024]{1,0:T(8,128)(2,1)S(1)}, bf16[128,1024]{1,0:T(8,128)(2,1)S(1)}, u32[]{:S(2)}, u32[]{:S(2)}) %collective-permute-start.93) | collective-permute-done | bytes 262176 | tf_op jit(solution)/shard_map/ppermute | solution.py:98
  13.7 0.0 copy-done.2
  13.7 0.0 copy-done.3
  13.7 0.8 %pad_maximum_fusion.32 = (bf16[256,512]{1,0:T(8,128)(2,1)}, bf16[256,512]{1,0:T(8,128)(2,1)}) fusion(bf16[128,512]{1,0:T(8,128)(2,1)S(1)} %copy-done.2, bf16[128,512]{1,0:T(8,128)(2,1)S(1)} %get-tuple-element.534, bf16[128,512]{1,0:T(8,128)(2,1)S(1)} %copy-done.3, bf16[128,512]{1,0:T(8,128)(2,1)S(1)} %get-tuple-element.533), kind=kLoop, calls=%fused_computation.94 | loop fusion | flops 1048576 | bytes 1048576 | tf_op jit(solution)/shard_map/concatenate | solution.py:99
  14.6 15.5 %shard_map.178 = (bf16[128,4096]{1,0:T(8,128)(2,1)S(1)}, f32[256,512]{1,0:T(8,128)S(1)}, f32[256,512]{1,0:T(8,128)S(1)}) custom-call(bf16[128,4096]{1,0:T(8,128)(2,1)} %q_ref.1, bf16[128,4096]{1,0:T(8,128)(2,1)} %do_ref.1, bf16[256,512]{1,0:T(8,128)(2,1)} %get-tuple-element.535.k_ref, bf16[256,512]{1,0:T(8,128)(2,1)} %get-tuple-element.536.v_ref, ...), custom_call_target="tpu_custom_call" | custom-call | tf_op jit(solution)/shard_map/pallas_call | solution.py:55
  30.1 35.0 %conditional.1 = (bf16[128,4096]{1,0:T(8,128)(2,1)}, bf16[128,512]{1,0:T(8,128)(2,1)S(1)}, bf16[128,512]{1,0:T(8,128)(2,1)S(1)}) conditional(s32[]{:T(128)} %bitcast, (bf16[128,4096]{1,0:T(8,128)(2,1)S(1)}, f32[256,512]{1,0:T(8,128)S(1)}, f32[256,512]{1,0:T(8,128)S(1)}) %shard_map.178, ...), branch_computations={%region_3.4_spmd, %region_4.5_spmd, %region_5.6_spmd, %region_6.7_... | conditional | flops 524288 | bytes 12320912 | solution.py:88
  30.2 0.1 fusion.34
  30.3 3.1 %collective-permute-start.4 = (f32[128,1024]{1,0:T(8,128)S(1)}, f32[128,1024]{1,0:T(8,128)S(1)}, u32[]{:S(2)}, u32[]{:S(2)}) collective-permute-start(f32[128,1024]{1,0:T(8,128)S(1)} %pad_maximum_fusion.1), channel_id=1, source_target_pairs={{1,0},{2,1},{3,2},{4,3},{5,4},{6,5},{7,6},{8,7},{9,8},{10,9},{11,1... | collective-permute-start | bytes 1572872 | tf_op jit(solution)/shard_map/cond/branch_1_fun/ppermute | solution.py:81
  33.4 3.8 %collective-permute-start.3 = (bf16[128,4096]{1,0:T(8,128)(2,1)S(1)}, bf16[128,4096]{1,0:T(8,128)(2,1)}, u32[]{:S(2)}, u32[]{:S(2)}) collective-permute-start(bf16[128,4096]{1,0:T(8,128)(2,1)S(1)} %get-tuple-element.189), channel_id=1, source_target_pairs={{0,32},{16,48},{32,0},{48,16},{64,96},{80,112},{96,64},{112,80},{1... | collective-permute-start | bytes 3145736 | tf_op jit(solution)/shard_map/cond/branch_1_fun/ppermute | solution.py:79
  37.2 7.8 %collective-permute-done.4 = f32[128,1024]{1,0:T(8,128)S(1)} collective-permute-done((f32[128,1024]{1,0:T(8,128)S(1)}, f32[128,1024]{1,0:T(8,128)S(1)}, u32[]{:S(2)}, u32[]{:S(2)}) %collective-permute-start.4) | collective-permute-done | bytes 524320 | tf_op jit(solution)/shard_map/cond/branch_1_fun/ppermute | solution.py:81
  45.0 0.1 fusion.1
  45.1 3.8 %collective-permute-start.5 = (bf16[128,1024]{1,0:T(8,128)(2,1)S(1)}, bf16[128,1024]{1,0:T(8,128)(2,1)S(1)}, u32[]{:S(2)}, u32[]{:S(2)}) collective-permute-start(bf16[128,1024]{1,0:T(8,128)(2,1)S(1)} %fusion.1), channel_id=1, source_target_pairs={{0,32},{16,48},{32,0},{48,16},{64,96},{80,112},{96,64},{112,80},{1... | collective-permute-start | bytes 786440 | tf_op jit(solution)/shard_map/cond/branch_1_fun/ppermute | solution.py:83
  48.9 16.0 %collective-permute-done.5 = bf16[128,1024]{1,0:T(8,128)(2,1)S(1)} collective-permute-done((bf16[128,1024]{1,0:T(8,128)(2,1)S(1)}, bf16[128,1024]{1,0:T(8,128)(2,1)S(1)}, u32[]{:S(2)}, u32[]{:S(2)}) %collective-permute-start.5) | collective-permute-done | bytes 262176 | tf_op jit(solution)/shard_map/cond/branch_1_fun/ppermute | solution.py:83
  64.9 0.0 collective-permute-done.3
  65.1 0.0 copy-start.4
  65.1 0.0 copy-start.5
  65.1 0.0 copy-start.1
  65.2 2.4 %copy.200 = bf16[128,4096]{1,0:T(8,128)(2,1)} copy(bf16[128,4096]{1,0:T(8,128)(2,1)} %get-tuple-element.633) | data formatting | bytes 2097152
  67.5 0.0 copy-done.4
  67.5 0.0 copy-done.5
  67.5 0.0 copy-done.1
  (7 shorter events, 0.1 us)
Async XLA Ops:
  0.6 4.5 %copy-start = (s32[32,32]{1,0:T(8,128)S(1)}, s32[32,32]{1,0:T(8,128)}, u32[]{:S(2)}) copy-start(s32[32,32]{1,0:T(8,128)} %param.41) | copy-start | bytes 12292
  1.6 12.0 %collective-permute-start.93 = (bf16[128,1024]{1,0:T(8,128)(2,1)S(1)}, bf16[128,1024]{1,0:T(8,128)(2,1)S(1)}, u32[]{:S(2)}, u32[]{:S(2)}) collective-permute-start(bf16[128,1024]{1,0:T(8,128)(2,1)S(1)} %pad_maximum_fusion.31), channel_id=1, source_target_pairs={{0,1},{1,2},{2,3},{3,4},{4,5},{5,6},{6,7},{7,8},{8,9},{9,10},{10,1... | collective-permute-start | bytes 786440 | tf_op jit(solution)/shard_map/ppermute | solution.py:98
  7.1 6.6 %copy-start.2 = (bf16[128,512]{1,0:T(8,128)(2,1)S(1)}, bf16[128,512]{1,0:T(8,128)(2,1)}, u32[]{:S(2)}) copy-start(bf16[128,512]{1,0:T(8,128)(2,1)} %param.38) | copy-start | bytes 393220
  7.1 6.7 %copy-start.3 = (bf16[128,512]{1,0:T(8,128)(2,1)S(1)}, bf16[128,512]{1,0:T(8,128)(2,1)}, u32[]{:S(2)}) copy-start(bf16[128,512]{1,0:T(8,128)(2,1)} %param.39) | copy-start | bytes 393220
  30.3 14.7 %collective-permute-start.4 = (f32[128,1024]{1,0:T(8,128)S(1)}, f32[128,1024]{1,0:T(8,128)S(1)}, u32[]{:S(2)}, u32[]{:S(2)}) collective-permute-start(f32[128,1024]{1,0:T(8,128)S(1)} %pad_maximum_fusion.1), channel_id=1, source_target_pairs={{1,0},{2,1},{3,2},{4,3},{5,4},{6,5},{7,6},{8,7},{9,8},{10,9},{11,1... | collective-permute-start | bytes 1572872 | tf_op jit(solution)/shard_map/cond/branch_1_fun/ppermute | solution.py:81
  33.4 31.5 %collective-permute-start.3 = (bf16[128,4096]{1,0:T(8,128)(2,1)S(1)}, bf16[128,4096]{1,0:T(8,128)(2,1)}, u32[]{:S(2)}, u32[]{:S(2)}) collective-permute-start(bf16[128,4096]{1,0:T(8,128)(2,1)S(1)} %get-tuple-element.189), channel_id=1, source_target_pairs={{0,32},{16,48},{32,0},{48,16},{64,96},{80,112},{96,64},{112,80},{1... | collective-permute-start | bytes 3145736 | tf_op jit(solution)/shard_map/cond/branch_1_fun/ppermute | solution.py:79
  45.1 19.8 %collective-permute-start.5 = (bf16[128,1024]{1,0:T(8,128)(2,1)S(1)}, bf16[128,1024]{1,0:T(8,128)(2,1)S(1)}, u32[]{:S(2)}, u32[]{:S(2)}) collective-permute-start(bf16[128,1024]{1,0:T(8,128)(2,1)S(1)} %fusion.1), channel_id=1, source_target_pairs={{0,32},{16,48},{32,0},{48,16},{64,96},{80,112},{96,64},{112,80},{1... | collective-permute-start | bytes 786440 | tf_op jit(solution)/shard_map/cond/branch_1_fun/ppermute | solution.py:83
  65.1 2.4 %copy-start.4 = (bf16[128,512]{1,0:T(8,128)(2,1)}, bf16[128,512]{1,0:T(8,128)(2,1)S(1)}, u32[]{:S(2)}) copy-start(bf16[128,512]{1,0:T(8,128)(2,1)S(1)} %get-tuple-element.635) | copy-start | bytes 393220
  65.1 2.4 %copy-start.5 = (bf16[128,512]{1,0:T(8,128)(2,1)}, bf16[128,512]{1,0:T(8,128)(2,1)S(1)}, u32[]{:S(2)}) copy-start(bf16[128,512]{1,0:T(8,128)(2,1)S(1)} %get-tuple-element.634) | copy-start | bytes 393220
  65.1 2.4 %copy-start.1 = (s32[32,32]{1,0:T(8,128)S(1)}, s32[32,32]{1,0:T(8,128)}, u32[]{:S(2)}) copy-start(s32[32,32]{1,0:T(8,128)} %param.41) | copy-start | bytes 12292
